TPU v7x, 256 devices: a whole 4x4x8 slice. The times are simulated.
256 devices in a mesh: dp: 8 (over x, core), seq: 32 (over y, z).
Axes of the slice: x: 4, y: 4, z: 8, core: 2. Of those that a mesh axis runs over, the one named last changes fastest.
Arguments:
- activations: bfloat16 [8, 4096, 2048], P('dp', 'seq'), may hold values from -16 to 16
- w_query: bfloat16 [2048, 2048], P('seq')
- w_key: bfloat16 [2048, 256], P('seq')
- w_value: bfloat16 [2048, 256], P('seq'), may hold values from -0.125 to 0.125
- key_blocks: int32 [32, 32, 7], replicated, may hold values from 0 to 31, as said below
- random_count: int32 [32], replicated, may hold values from 1 to 3, 64 in all
- grad_out: bfloat16 [8, 4096, 2048], P('dp', 'seq'), may hold values from -6 to 6
Outputs:
- attn_out: bfloat16 [8, 4096, 2048], P('dp', 'seq')
- grad_x: bfloat16 [8, 4096, 2048], P('dp', 'seq')
- grad_wq: bfloat16 [2048, 2048], P('seq')
- grad_wk: bfloat16 [2048, 256], P('seq')
- grad_wv: bfloat16 [2048, 256], P('seq')
Inputs may be any that keep to these rules, and one draw needn't show every extreme that they name: `key_blocks`: row b of head h: columns 0 to 2 are b - 1, b and b + 1 modulo 32; column 3 is one block of the head, the same in all its rows; columns 4 to 6 are three blocks that differ from each other and from the row's first four entries. Head h uses the first random_count[h] of its three random key blocks; the counts sum to 64.
All inputs are finite; a program needn't handle non-finite values.
Results may differ from a plain program's by a relative error of at most 0.025.
The roundings to bfloat16 on the way count: a program that leaves them out, or rounds other values in their place, can miss the bound.
Values may be sent and summed in bfloat16 or wider, within the bound.
No kernel may reach another device: no remote copies, remote signals or barrier semaphores. Data moves between devices by JAX's collectives and lax.ppermute only.
A program may use at most 128 MiB of HBM per device.

v0:
```python
import math
import jax
import jax.numpy as jnp
from jax import lax
from jax.sharding import PartitionSpec as P

HD = 64
GROUP = 8
masked_score = -1e30
query_group = 4
RING_Z = 8


def head_pass(queries, key_rows, value_rows, grad_head, blocks, extra_count):
    seq_len, head_width = queries.shape
    block_count, slot_count = blocks.shape
    block_len = seq_len // block_count
    score_scale = head_width ** (-0.5)
    key_tiles = key_rows.reshape(block_count, block_len, head_width)
    value_tiles = value_rows.reshape(block_count, block_len, head_width)
    q_part = queries.reshape(block_count, block_len, head_width)
    g_part = grad_head.reshape(block_count, block_len, head_width)
    usable = jnp.repeat(jnp.arange(slot_count) < 4 + extra_count, block_len)
    k_part = key_tiles[blocks].reshape(block_count, slot_count * block_len, head_width)
    v_part = value_tiles[blocks].reshape(block_count, slot_count * block_len, head_width)
    scores = (
        jnp.einsum("gqe,gke->gqk", q_part, k_part, preferred_element_type=jnp.float32) * score_scale
    )
    scores = jnp.where(usable, scores, masked_score)
    highest = jnp.max(scores, axis=-1, keepdims=True)
    exponent = jnp.exp(scores - highest)
    shares = exponent / jnp.sum(exponent, axis=-1, keepdims=True)
    shares_low = shares.astype(jnp.bfloat16)
    attended = jnp.einsum(
        "gqk,gke->gqe", shares_low, v_part, preferred_element_type=jnp.float32
    ).astype(jnp.bfloat16)
    grad_shares = jnp.einsum("gqe,gke->gqk", g_part, v_part, preferred_element_type=jnp.float32)
    weighted = jnp.sum(grad_shares * shares, axis=-1, keepdims=True)
    grad_scores = (shares * (grad_shares - weighted)).astype(jnp.bfloat16)
    grad_query = (
        jnp.einsum("gqk,gke->gqe", grad_scores, k_part, preferred_element_type=jnp.float32)
        * score_scale
    ).astype(jnp.bfloat16)
    grad_keys = (
        jnp.einsum("gqk,gqe->gke", grad_scores, q_part, preferred_element_type=jnp.float32)
        * score_scale
    )
    grad_values = jnp.einsum("gqk,gqe->gke", shares_low, g_part, preferred_element_type=jnp.float32)
    pieces = jnp.concatenate([grad_keys, grad_values], axis=-1).reshape(
        block_count * slot_count, block_len * 2 * head_width
    )
    owner = (
        blocks.reshape(1, block_count * slot_count)
        == jnp.arange(block_count, dtype=blocks.dtype)[:, None]
    ).astype(jnp.float32)
    summed = jnp.dot(owner, pieces, precision=lax.Precision.HIGHEST)
    return (
        attended.reshape(seq_len, head_width),
        grad_query.reshape(seq_len, head_width),
        summed.reshape(seq_len, 2 * head_width),
    )


def ring_reduce_scatter(parts, ring, stride, position):
    seq_devices = lax.axis_size("seq")
    group = ring * stride
    me = position // stride % ring
    width = parts.shape[-1] // 2
    ahead = [
        (s, s // group * group + (s // stride % ring + 1) % ring * stride + s % stride)
        for s in range(seq_devices)
    ]
    behind = [(b, a) for a, b in ahead]
    total = []
    for side, perm, sign in ((0, ahead, 1), (1, behind, -1)):
        own = parts[..., side * width : (side + 1) * width]

        def chunk(k):
            return lax.dynamic_index_in_dim(own, (me - sign * (1 + k)) % ring, 0, keepdims=False)

        buf = chunk(0)
        for k in range(ring - 1):
            got = lax.ppermute(buf, "seq", perm)
            buf = (got.astype(jnp.float32) + chunk(k + 1).astype(jnp.float32)).astype(jnp.bfloat16)
        total.append(buf)
    return jnp.concatenate(total, axis=-1)


def per_device(activations, w_query, w_key, w_value, key_blocks, random_count, grad_out):
    seq_devices = lax.axis_size("seq")
    dp_devices = lax.axis_size("dp")
    position = lax.axis_index("seq")
    dp_index = lax.axis_index("dp")
    tokens = activations[0]
    grad_rows = grad_out[0]
    tok_count = tokens.shape[0]
    heads = w_query.shape[1] // HD
    kv_heads = w_key.shape[1] // HD
    query_cols = heads * HD
    kv_cols = kv_heads * HD
    all_cols = query_cols + 2 * kv_cols
    w_local = jnp.concatenate([w_query, w_key, w_value], axis=1)
    w_full = lax.all_gather(w_local, "seq", axis=0, tiled=True)
    projected = jnp.dot(tokens, w_full, preferred_element_type=jnp.float32).astype(jnp.bfloat16)
    queries = projected[:, :query_cols]
    key_proj = projected[:, query_cols : query_cols + kv_cols]
    value_proj = projected[:, query_cols + kv_cols :]
    query_pieces = queries.reshape(tok_count, heads, HD).transpose(1, 0, 2)
    grad_pieces = grad_rows.reshape(tok_count, heads, HD).transpose(1, 0, 2)
    paired = jnp.concatenate(
        [key_proj.reshape(tok_count, kv_heads, HD), value_proj.reshape(tok_count, kv_heads, HD)],
        axis=2,
    )
    kv_pieces = jnp.repeat(paired.transpose(1, 0, 2), GROUP, axis=0)
    sent = jnp.concatenate([query_pieces, grad_pieces, kv_pieces], axis=2)
    landed = lax.all_to_all(sent, "seq", split_axis=0, concat_axis=1, tiled=True)[0]
    head_q = landed[:, :HD]
    head_grad = landed[:, HD : 2 * HD]
    head_k = landed[:, 2 * HD : 3 * HD]
    head_v = landed[:, 3 * HD :]
    blocks_mine = lax.dynamic_index_in_dim(key_blocks, position, 0, keepdims=False)
    count_mine = lax.dynamic_index_in_dim(random_count, position, 0, keepdims=False)
    attended, grad_query, grad_kv = head_pass(
        head_q, head_k, head_v, head_grad, blocks_mine, count_mine
    )
    back_sent = jnp.concatenate(
        [
            attended.reshape(seq_devices, tok_count, HD),
            grad_query.reshape(seq_devices, tok_count, HD),
            grad_kv.astype(jnp.bfloat16).reshape(seq_devices, tok_count, 2 * HD),
        ],
        axis=2,
    )
    back = lax.all_to_all(back_sent, "seq", split_axis=0, concat_axis=0, tiled=True)
    back_out = back[:, :, :HD]
    back_query = back[:, :, HD : 2 * HD]
    back_kv = back[:, :, 2 * HD :]
    out_rows = back_out.transpose(1, 0, 2).reshape(tok_count, heads * HD)
    grad_q_rows = back_query.transpose(1, 0, 2).reshape(tok_count, heads * HD)
    kv_sum = jnp.sum(
        back_kv.reshape(kv_heads, GROUP, tok_count, 2 * HD), axis=1, dtype=jnp.float32
    ).astype(jnp.bfloat16)
    grad_k_rows = kv_sum[:, :, :HD].transpose(1, 0, 2).reshape(tok_count, kv_heads * HD)
    grad_v_rows = kv_sum[:, :, HD:].transpose(1, 0, 2).reshape(tok_count, kv_heads * HD)
    combined = jnp.concatenate([grad_q_rows, grad_k_rows, grad_v_rows], axis=1)
    contract = (((1,), (1,)), ((), ()))
    grad_x_rows = lax.dot_general(
        combined, w_full, contract, preferred_element_type=jnp.float32
    ).astype(jnp.bfloat16)
    factor = 1.0 / math.sqrt(tok_count * seq_devices * dp_devices)
    over_tokens = (((0,), (0,)), ((), ()))
    term = (
        lax.dot_general(tokens, combined, over_tokens, preferred_element_type=jnp.float32) * factor
    ).astype(jnp.bfloat16)
    half = all_cols // 2
    core = dp_index % 2
    pairs = [(i, i ^ 1) for i in range(dp_devices)]
    keep = lax.dynamic_slice_in_dim(term, core * half, half, axis=1)
    give = lax.dynamic_slice_in_dim(term, (1 - core) * half, half, axis=1)
    got = lax.ppermute(give, "dp", pairs)
    chip_sum = (keep.astype(jnp.float32) + got.astype(jnp.float32)).astype(jnp.bfloat16)
    rows = chip_sum.shape[0] // seq_devices
    by_z = chip_sum.reshape(seq_devices // RING_Z, RING_Z, rows, half).transpose(1, 0, 2, 3)
    by_y = ring_reduce_scatter(by_z, RING_Z, 1, position)
    part = ring_reduce_scatter(by_y, seq_devices // RING_Z, RING_Z, position)
    step = 2
    while step < dp_devices:
        mates = [(i, i ^ step) for i in range(dp_devices)]
        other = lax.ppermute(part, "dp", mates)
        part = (part.astype(jnp.float32) + other.astype(jnp.float32)).astype(jnp.bfloat16)
        step *= 2
    other_half = lax.ppermute(part, "dp", pairs)
    first = jnp.where(core == 0, part, other_half)
    second = jnp.where(core == 0, other_half, part)
    grad_all = jnp.concatenate([first, second], axis=1)
    grad_wq = grad_all[:, :query_cols]
    grad_wk = grad_all[:, query_cols : query_cols + kv_cols]
    grad_wv = grad_all[:, query_cols + kv_cols :]
    return (out_rows[None], grad_x_rows[None], grad_wq, grad_wk, grad_wv)


def solution(mesh):
    placed = (
        P("dp", "seq", None),
        P("seq", None),
        P("seq", None),
        P("seq", None),
        P(),
        P(),
        P("dp", "seq", None),
    )
    return jax.shard_map(
        per_device,
        mesh=mesh,
        in_specs=placed,
        out_specs=(
            P("dp", "seq", None),
            P("dp", "seq", None),
            P("seq", None),
            P("seq", None),
            P("seq", None),
        ),
        check_vma=False,
    )
```

profile of v0, /device:TPU:1, one launch (start us, length us, event | category | flops | bytes accessed | tf_op | source)
XLA Modules:
  0.0 566.1 jit_solution(12210671963242412984)
XLA Ops:
  10.4 113.4 %all-gather.2.cloned.1.call-done = bf16[2048,2560]{1,0:T(8,128)(2,1)} async-done(((bf16[64,2560]{1,0:T(8,128)(2,1)}), bf16[2048,2560]{1,0:T(8,128)(2,1)}) %all-gather.2.cloned.1.call-update) | async-done | bytes 10485776 | tf_op jit(solution)/shard_map/all_gather | solution.py:103
  123.7 6.9 %fusion.13 = bf16[128,2560]{0,1:T(8,128)(2,1)S(1)} fusion(bf16[2048,2560]{1,0:T(8,128)(2,1)} %all-gather.2.cloned.1.call-done, bf16[1,128,2048]{2,1,0:T(8,128)(2,1)S(1)} %copy-done), kind=kOutput, calls=%fused_computation.27 | convolution fusion | flops 1342504960 | bytes 11665408 | tf_op jit(solution)/shard_map/dot_general | solution.py:104
  132.5 5.6 all-to-all-start
  140.7 46.1 %all-to-all-done = bf16[32,128,256]{1,2,0:T(8,128)(2,1)} async-done(((bf16[32,128,256]{1,2,0:T(8,128)(2,1)}), bf16[32,128,256]{1,2,0:T(8,128)(2,1)}, u32[]{:S(2)}, u32[]{:S(2)}) %all-to-all-start) | async-done | bytes 2097184 | tf_op jit(solution)/shard_map/all_to_all | solution.py:116
  186.7 3.3 copy.117
  190.0 2.7 fusion.73
  195.9 2.9 gather_fusion
  198.8 6.2 %copy.122 = bf16[224,128,64]{1,0,2:T(8,128)(2,1)} copy(bf16[224,128,64]{1,2,0:T(8,128)(2,1)} %gather_fusion) | data formatting | bytes 7340032 | tf_op jit(solution)/shard_map/gather | solution.py:24
  205.0 7.8 %reshape.152 = bf16[32,896,64]{1,0,2:T(8,128)(2,1)} reshape(bf16[224,128,64]{1,0,2:T(8,128)(2,1)} %copy.122) | data formatting | bytes 7340032 | tf_op jit(solution)/shard_map/reshape | solution.py:24
  212.8 3.0 gather_fusion.1
  215.8 6.2 %copy.127 = bf16[224,128,64]{1,0,2:T(8,128)(2,1)} copy(bf16[224,128,64]{1,2,0:T(8,128)(2,1)} %gather_fusion.1) | data formatting | bytes 7340032 | tf_op jit(solution)/shard_map/gather | solution.py:25
  222.0 7.8 %reshape.154 = bf16[32,896,64]{1,0,2:T(8,128)(2,1)} reshape(bf16[224,128,64]{1,0,2:T(8,128)(2,1)} %copy.127) | data formatting | bytes 7340032 | tf_op jit(solution)/shard_map/reshape | solution.py:25
  229.8 10.8 %fusion.77 = (f32[32,128]{1,0:T(8,128)S(1)}, f32[32,128,896]{2,1,0:T(8,128)}) fusion(pred[896]{0:T(1024)(128)(4,1)S(1)} %broadcast_bitcast_fusion, bf16[32,128,64]{2,1,0:T(8,128)(2,1)S(1)} %bitcast.152, bf16[32,896,64]{1,0,2:T(8,128)(2,1)} %reshape.152), kind=kOutput, calls=%fused_computation.119 | convolution fusion | flops 484443008 | bytes 18891648 | tf_op jit(solution)/shard_map/sub | solution.py:31
  240.6 9.3 %fusion.31 = bf16[32,128,64]{1,2,0:T(8,128)(2,1)S(1)} fusion(bf16[32,896,64]{1,0,2:T(8,128)(2,1)} %reshape.154, f32[32,128,896]{2,1,0:T(8,128)} %get-tuple-element.49, f32[32,128]{1,0:T(8,128)S(1)} %get-tuple-element.48), kind=kOutput, calls=%fused_computation.42 | convolution fusion | flops 477364224 | bytes 18890752 | tf_op jit(solution)/shard_map/gqk,gke->gqe/dot_general | solution.py:34
  249.9 9.8 %fusion.9 = f32[32,896,64]{1,2,0:T(8,128)} fusion(bf16[32,128,64]{2,1,0:T(8,128)(2,1)S(1)} %bitcast.162, f32[32,128,896]{2,1,0:T(8,128)} %get-tuple-element.49, f32[32,128]{1,0:T(8,128)S(1)} %get-tuple-element.48), kind=kOutput, calls=%fused_computation.22 | convolution fusion | flops 477102080 | bytes 22560768 | tf_op jit(solution)/shard_map/gqk,gqe->gke/dot_general | solution.py:48
  259.7 11.0 %multiply_reduce_fusion = (f32[32,128]{1,0:T(8,128)S(1)}, f32[32,128,896]{2,1,0:T(8,128)}) fusion(f32[32,128,896]{2,1,0:T(8,128)} %get-tuple-element.49, f32[32,128]{1,0:T(8,128)S(1)} %get-tuple-element.48, bf16[32,128,64]{2,1,0:T(8,128)(2,1)S(1)} %bitcast.163, bf16[32,896,64]{1,0,2:T(8,128)(2,1)S(1)} %copy-done.7), kind=kOutput, calls=%fused_computation.9 | convolution fusion | flops 480768000 | bytes 33587200 | tf_op jit(solution)/shard_map/gqe,gke->gqk/dot_general | solution.py:37
  270.7 10.8 %multiply_convert_fusion.1 = bf16[32,128,896]{2,1,0:T(8,128)(2,1)S(1)} fusion(f32[32,128,896]{2,1,0:T(8,128)} %get-tuple-element.51, f32[32,128]{1,0:T(8,128)S(1)} %get-tuple-element.50, f32[32,128,896]{2,1,0:T(8,128)} %get-tuple-element.49, f32[32,128]{1,0:T(8,128)S(1)} %get-tuple-element.48), kind=kLoop, calls=%fused_computation.8 | loop fusion | flops 14680064 | bytes 36732928 | tf_op jit(solution)/shard_map/convert_element_type | solution.py:39
  281.5 3.4 fusion.28
  284.8 4.3 broadcast_multiply_fusion
  290.8 10.5 %pad_maximum_fusion = f32[32,896,128]{1,2,0:T(8,128)} fusion(f32[32,896,64]{1,2,0:T(8,128)} %fusion.9, f32[32,896,64]{1,2,0:T(8,128)} %broadcast_multiply_fusion), kind=kLoop, calls=%fused_computation.7 | loop fusion | flops 3670016 | bytes 29360128 | tf_op jit(solution)/shard_map/concatenate | solution.py:49
  301.3 16.1 %copy.136 = f32[32,896,128]{2,1,0:T(8,128)} copy(f32[32,896,128]{1,2,0:T(8,128)} %pad_maximum_fusion) | data formatting | bytes 29360128 | tf_op jit(solution)/shard_map/concatenate | solution.py:49
  317.4 16.0 %reshape.156 = f32[224,16384]{1,0:T(8,128)} reshape(f32[32,896,128]{2,1,0:T(8,128)} %copy.136) | data formatting | bytes 29360128 | tf_op jit(solution)/shard_map/reshape | solution.py:49
  335.1 9.1 %fusion.22 = bf16[32,128,128]{2,0,1:T(8,128)(2,1)S(1)} fusion(s32[224]{0:T(256)S(1)} %eq.47, f32[224,16384]{1,0:T(8,128)} %reshape.156), kind=kOutput, calls=%fused_computation.39 | convolution fusion | flops 1409817600 | bytes 15729536 | tf_op jit(solution)/shard_map/dot_general | solution.py:56
  345.3 2.5 copy.140
  347.9 7.1 %all-to-all-start.1 = ((bf16[32,128,256]{2,1,0:T(8,128)(2,1)}), bf16[32,128,256]{2,1,0:T(8,128)(2,1)S(1)}, u32[]{:S(2)}, u32[]{:S(2)}) async-start(bf16[32,128,256]{2,1,0:T(8,128)(2,1)} %copy.140), calls=%async_computation.1 | async-start | bytes 4194304 | tf_op jit(solution)/shard_map/all_to_all | solution.py:134
  355.0 48.6 %all-to-all-done.1 = bf16[32,128,256]{2,1,0:T(8,128)(2,1)S(1)} async-done(((bf16[32,128,256]{2,1,0:T(8,128)(2,1)}), bf16[32,128,256]{2,1,0:T(8,128)(2,1)S(1)}, u32[]{:S(2)}, u32[]{:S(2)}) %all-to-all-start.1) | async-done | bytes 2097184 | tf_op jit(solution)/shard_map/all_to_all | solution.py:134
  403.7 1.9 fusion.72
  407.9 4.2 multiply_convert_fusion
  412.2 2.9 dynamic-slice_bitcast_fusion
  415.1 2.7 copy-done.1
  417.8 2.5 collective-permute-start
  420.3 8.6 %collective-permute-done = bf16[2048,1280]{1,0:T(8,128)(2,1)} collective-permute-done((bf16[2048,1280]{1,0:T(8,128)(2,1)}, bf16[2048,1280]{1,0:T(8,128)(2,1)}, u32[]{:S(2)}, u32[]{:S(2)}) %collective-permute-start) | collective-permute-done | bytes 5242912 | tf_op jit(solution)/shard_map/ppermute | solution.py:160
  428.9 5.4 fusion.5
  439.9 7.0 %collective-permute-done.11 = bf16[4,64,640]{2,1,0:T(8,128)(2,1)} collective-permute-done((bf16[4,64,640]{2,1,0:T(8,128)(2,1)}, bf16[4,64,640]{2,1,0:T(8,128)(2,1)}, u32[]{:S(2)}, u32[]{:S(2)}) %collective-permute-start.11) | collective-permute-done | bytes 327712 | tf_op jit(solution)/shard_map/ppermute | solution.py:83
  446.9 1.9 fusion.46
  448.8 1.9 collective-permute-start.12
  450.7 1.8 fusion.53
  452.5 4.8 collective-permute-done.12
  457.3 1.9 fusion.45
  459.2 2.9 collective-permute-start.13
  462.1 1.8 fusion.52
  463.9 3.4 collective-permute-done.13
  467.3 1.9 fusion.44
  469.2 3.4 collective-permute-start.14
  472.6 1.8 fusion.51
  474.4 2.5 collective-permute-done.14
  476.9 1.9 fusion.43
  478.8 3.1 collective-permute-start.15
  483.7 2.5 collective-permute-done.15
  486.2 1.9 fusion.42
  488.1 3.1 collective-permute-start.16
  493.0 2.5 collective-permute-done.16
  495.6 1.9 fusion.41
  497.4 3.1 collective-permute-start.17
  501.7 3.2 collective-permute-done.17
  506.1 2.4 collective-permute-start.18
  511.3 2.1 collective-permute-start.19
  515.2 3.0 collective-permute-start.20
  519.8 4.4 collective-permute-done.10
  525.5 3.3 collective-permute-done.21
  528.8 2.8 collective-permute-start.22
  531.6 3.0 collective-permute-done.22
  534.7 13.0 %collective-permute-start.23 = (bf16[64,1280]{1,0:T(8,128)(2,1)S(1)}, bf16[64,1280]{1,0:T(8,128)(2,1)S(1)}, u32[]{:S(2)}, u32[]{:S(2)}) collective-permute-start(bf16[64,1280]{1,0:T(8,128)(2,1)S(1)} %add_convert_fusion), channel_id=1, source_target_pairs={{0,32},{32,0},{64,96},{96,64},{128,160},{160,128},{192,224},{224,1... | collective-permute-start | bytes 491528 | tf_op jit(solution)/shard_map/ppermute | solution.py:172
  547.7 8.5 %fusion.21 = bf16[1,128,2048]{2,1,0:T(8,128)(2,1)} fusion(bf16[2048,2560]{1,0:T(8,128)(2,1)} %all-gather.2.cloned.1.call-done, bf16[128,256]{0,1:T(8,128)(2,1)S(1)} %bitcast.165, bf16[128,256]{0,1:T(8,128)(2,1)S(1)} %bitcast.167, bf16[128,2048]{0,1:T(8,128)(2,1)} %bitcast.155), kind=kOutput, calls=%fused_computation.36 | convolution fusion | flops 1344405504 | bytes 11665408 | tf_op jit(solution)/shard_map/dot_general | solution.py:147
  (100 shorter events, 38.5 us)
Async XLA Ops:
  7.2 116.6 %copy-start = (bf16[1,128,2048]{2,1,0:T(8,128)(2,1)S(1)}, bf16[1,128,2048]{2,1,0:T(8,128)(2,1)}, u32[]{:S(2)}) copy-start(bf16[1,128,2048]{2,1,0:T(8,128)(2,1)} %param.7) | copy-start | bytes 1572868
  7.2 116.6 %all-gather.2.cloned.1.call-start = ((), (), s32[]{:S(2)}) async-start(), calls=%async_computation.2 | async-start | bytes 10813440 | tf_op jit(solution)/shard_map/all_gather | solution.py:103
  130.7 7.5 %copy-start.10 = (s32[32]{0:T(128)S(1)}, s32[32]{0:T(128)}, u32[]{:S(2)}) copy-start(s32[32]{0:T(128)} %param.12) | copy-start | bytes 388
  132.5 54.2 %all-to-all-start = ((bf16[32,128,256]{1,2,0:T(8,128)(2,1)}), bf16[32,128,256]{1,2,0:T(8,128)(2,1)}, u32[]{:S(2)}, u32[]{:S(2)}) async-start(bf16[32,128,256]{1,2,0:T(8,128)(2,1)} %pad_maximum_fusion.1), calls=%async_computation | async-start | bytes 4194304 | tf_op jit(solution)/shard_map/all_to_all | solution.py:116
  222.0 7.8 %copy-start.3 = (bf16[4096,64]{1,0:T(8,128)(2,1)S(1)}, bf16[4096,64]{1,0:T(8,128)(2,1)}, u32[]{:S(2)}) copy-start(bf16[4096,64]{1,0:T(8,128)(2,1)} %get-tuple-element.39) | copy-start | bytes 1572868
  240.6 9.3 %copy-start.8 = (bf16[4096,64]{1,0:T(8,128)(2,1)S(1)}, bf16[4096,64]{1,0:T(8,128)(2,1)}, u32[]{:S(2)}) copy-start(bf16[4096,64]{1,0:T(8,128)(2,1)} %get-tuple-element.37) | copy-start | bytes 1572868
  249.9 9.8 %copy-start.7 = (bf16[32,896,64]{1,0,2:T(8,128)(2,1)S(1)}, bf16[32,896,64]{1,0,2:T(8,128)(2,1)}, u32[]{:S(2)}) copy-start(bf16[32,896,64]{1,0,2:T(8,128)(2,1)} %reshape.154) | copy-start | bytes 11010052
  270.7 10.8 %copy-start.6 = (bf16[32,896,64]{1,0,2:T(8,128)(2,1)S(1)}, bf16[32,896,64]{1,0,2:T(8,128)(2,1)}, u32[]{:S(2)}) copy-start(bf16[32,896,64]{1,0,2:T(8,128)(2,1)} %reshape.152) | copy-start | bytes 11010052
  317.4 16.1 %copy-start.9 = (bf16[32,128,64]{1,2,0:T(8,128)(2,1)S(1)}, bf16[32,128,64]{1,2,0:T(8,128)(2,1)}, u32[]{:S(2)}) copy-start(bf16[32,128,64]{1,2,0:T(8,128)(2,1)} %fusion.28) | copy-start | bytes 1572868
  347.9 55.8 %all-to-all-start.1 = ((bf16[32,128,256]{2,1,0:T(8,128)(2,1)}), bf16[32,128,256]{2,1,0:T(8,128)(2,1)S(1)}, u32[]{:S(2)}, u32[]{:S(2)}) async-start(bf16[32,128,256]{2,1,0:T(8,128)(2,1)} %copy.140), calls=%async_computation.1 | async-start | bytes 4194304 | tf_op jit(solution)/shard_map/all_to_all | solution.py:134
  407.2 5.0 copy-start.4
  412.1 5.7 %copy-start.1 = (bf16[2560,2048]{0,1:T(8,128)(2,1)}, bf16[2560,2048]{0,1:T(8,128)(2,1)S(1)}, u32[]{:S(2)}) copy-start(bf16[2560,2048]{0,1:T(8,128)(2,1)S(1)} %multiply_convert_fusion) | copy-start | bytes 31457284
  417.8 11.1 %collective-permute-start = (bf16[2048,1280]{1,0:T(8,128)(2,1)}, bf16[2048,1280]{1,0:T(8,128)(2,1)}, u32[]{:S(2)}, u32[]{:S(2)}) collective-permute-start(bf16[2048,1280]{1,0:T(8,128)(2,1)} %dynamic-slice_bitcast_fusion), channel_id=1, source_target_pairs={{0,32},{32,0},{64,96},{96,64},{128,160},{160,128},{192,224},{224,1... | collective-permute-start | bytes 15728648 | tf_op jit(solution)/shard_map/ppermute | solution.py:160
  435.4 1.5 copy-start.2
  437.7 9.2 %collective-permute-start.11 = (bf16[4,64,640]{2,1,0:T(8,128)(2,1)}, bf16[4,64,640]{2,1,0:T(8,128)(2,1)}, u32[]{:S(2)}, u32[]{:S(2)}) collective-permute-start(bf16[4,64,640]{2,1,0:T(8,128)(2,1)} %dynamic-slice_bitcast_fusion.1), channel_id=1, source_target_pairs={{1,0},{2,1},{3,2},{4,3},{5,4},{6,5},{7,6},{0,7},{9,8},{10,9},{11,1... | collective-permute-start | bytes 983048 | tf_op jit(solution)/shard_map/ppermute | solution.py:83
  438.9 11.7 %collective-permute-start.1 = (bf16[4,64,640]{2,1,0:T(8,128)(2,1)}, bf16[4,64,640]{2,1,0:T(8,128)(2,1)}, u32[]{:S(2)}, u32[]{:S(2)}) collective-permute-start(bf16[4,64,640]{2,1,0:T(8,128)(2,1)} %dynamic-slice_bitcast_fusion.2), channel_id=1, source_target_pairs={{0,1},{1,2},{2,3},{3,4},{4,5},{5,6},{6,7},{7,0},{8,9},{9,10},{10,1... | collective-permute-start | bytes 983048 | tf_op jit(solution)/shard_map/ppermute | solution.py:83
  448.8 8.5 %collective-permute-start.12 = (bf16[4,64,640]{2,1,0:T(8,128)(2,1)}, bf16[4,64,640]{2,1,0:T(8,128)(2,1)}, u32[]{:S(2)}, u32[]{:S(2)}) collective-permute-start(bf16[4,64,640]{2,1,0:T(8,128)(2,1)} %fusion.46), channel_id=1, source_target_pairs={{1,0},{2,1},{3,2},{4,3},{5,4},{6,5},{7,6},{0,7},{9,8},{10,9},{11,1... | collective-permute-start | bytes 983048 | tf_op jit(solution)/shard_map/ppermute | solution.py:83
  452.5 9.6 %collective-permute-start.2 = (bf16[4,64,640]{2,1,0:T(8,128)(2,1)}, bf16[4,64,640]{2,1,0:T(8,128)(2,1)}, u32[]{:S(2)}, u32[]{:S(2)}) collective-permute-start(bf16[4,64,640]{2,1,0:T(8,128)(2,1)} %fusion.53), channel_id=1, source_target_pairs={{0,1},{1,2},{2,3},{3,4},{4,5},{5,6},{6,7},{7,0},{8,9},{9,10},{10,1... | collective-permute-start | bytes 983048 | tf_op jit(solution)/shard_map/ppermute | solution.py:83
  459.2 8.1 %collective-permute-start.13 = (bf16[4,64,640]{2,1,0:T(8,128)(2,1)}, bf16[4,64,640]{2,1,0:T(8,128)(2,1)}, u32[]{:S(2)}, u32[]{:S(2)}) collective-permute-start(bf16[4,64,640]{2,1,0:T(8,128)(2,1)} %fusion.45), channel_id=1, source_target_pairs={{1,0},{2,1},{3,2},{4,3},{5,4},{6,5},{7,6},{0,7},{9,8},{10,9},{11,1... | collective-permute-start | bytes 983048 | tf_op jit(solution)/shard_map/ppermute | solution.py:83
  463.9 8.7 %collective-permute-start.3 = (bf16[4,64,640]{2,1,0:T(8,128)(2,1)}, bf16[4,64,640]{2,1,0:T(8,128)(2,1)}, u32[]{:S(2)}, u32[]{:S(2)}) collective-permute-start(bf16[4,64,640]{2,1,0:T(8,128)(2,1)} %fusion.52), channel_id=1, source_target_pairs={{0,1},{1,2},{2,3},{3,4},{4,5},{5,6},{6,7},{7,0},{8,9},{9,10},{10,1... | collective-permute-start | bytes 983048 | tf_op jit(solution)/shard_map/ppermute | solution.py:83
  469.2 7.7 %collective-permute-start.14 = (bf16[4,64,640]{2,1,0:T(8,128)(2,1)}, bf16[4,64,640]{2,1,0:T(8,128)(2,1)}, u32[]{:S(2)}, u32[]{:S(2)}) collective-permute-start(bf16[4,64,640]{2,1,0:T(8,128)(2,1)} %fusion.44), channel_id=1, source_target_pairs={{1,0},{2,1},{3,2},{4,3},{5,4},{6,5},{7,6},{0,7},{9,8},{10,9},{11,1... | collective-permute-start | bytes 983048 | tf_op jit(solution)/shard_map/ppermute | solution.py:83
  474.4 7.5 %collective-permute-start.4 = (bf16[4,64,640]{2,1,0:T(8,128)(2,1)}, bf16[4,64,640]{2,1,0:T(8,128)(2,1)}, u32[]{:S(2)}, u32[]{:S(2)}) collective-permute-start(bf16[4,64,640]{2,1,0:T(8,128)(2,1)} %fusion.51), channel_id=1, source_target_pairs={{0,1},{1,2},{2,3},{3,4},{4,5},{5,6},{6,7},{7,0},{8,9},{9,10},{10,1... | collective-permute-start | bytes 983048 | tf_op jit(solution)/shard_map/ppermute | solution.py:83
  478.8 7.5 %collective-permute-start.15 = (bf16[4,64,640]{2,1,0:T(8,128)(2,1)}, bf16[4,64,640]{2,1,0:T(8,128)(2,1)}, u32[]{:S(2)}, u32[]{:S(2)}) collective-permute-start(bf16[4,64,640]{2,1,0:T(8,128)(2,1)} %fusion.43), channel_id=1, source_target_pairs={{1,0},{2,1},{3,2},{4,3},{5,4},{6,5},{7,6},{0,7},{9,8},{10,9},{11,1... | collective-permute-start | bytes 983048 | tf_op jit(solution)/shard_map/ppermute | solution.py:83
  483.7 7.5 %collective-permute-start.5 = (bf16[4,64,640]{2,1,0:T(8,128)(2,1)}, bf16[4,64,640]{2,1,0:T(8,128)(2,1)}, u32[]{:S(2)}, u32[]{:S(2)}) collective-permute-start(bf16[4,64,640]{2,1,0:T(8,128)(2,1)} %fusion.50), channel_id=1, source_target_pairs={{0,1},{1,2},{2,3},{3,4},{4,5},{5,6},{6,7},{7,0},{8,9},{9,10},{10,1... | collective-permute-start | bytes 983048 | tf_op jit(solution)/shard_map/ppermute | solution.py:83
  488.1 7.5 %collective-permute-start.16 = (bf16[4,64,640]{2,1,0:T(8,128)(2,1)}, bf16[4,64,640]{2,1,0:T(8,128)(2,1)}, u32[]{:S(2)}, u32[]{:S(2)}) collective-permute-start(bf16[4,64,640]{2,1,0:T(8,128)(2,1)} %fusion.42), channel_id=1, source_target_pairs={{1,0},{2,1},{3,2},{4,3},{5,4},{6,5},{7,6},{0,7},{9,8},{10,9},{11,1... | collective-permute-start | bytes 983048 | tf_op jit(solution)/shard_map/ppermute | solution.py:83
  493.0 7.5 %collective-permute-start.6 = (bf16[4,64,640]{2,1,0:T(8,128)(2,1)}, bf16[4,64,640]{2,1,0:T(8,128)(2,1)}, u32[]{:S(2)}, u32[]{:S(2)}) collective-permute-start(bf16[4,64,640]{2,1,0:T(8,128)(2,1)} %fusion.49), channel_id=1, source_target_pairs={{0,1},{1,2},{2,3},{3,4},{4,5},{5,6},{6,7},{7,0},{8,9},{9,10},{10,1... | collective-permute-start | bytes 983048 | tf_op jit(solution)/shard_map/ppermute | solution.py:83
  497.4 7.5 %collective-permute-start.17 = (bf16[4,64,640]{2,1,0:T(8,128)(2,1)}, bf16[4,64,640]{2,1,0:T(8,128)(2,1)}, u32[]{:S(2)}, u32[]{:S(2)}) collective-permute-start(bf16[4,64,640]{2,1,0:T(8,128)(2,1)} %fusion.41), channel_id=1, source_target_pairs={{1,0},{2,1},{3,2},{4,3},{5,4},{6,5},{7,6},{0,7},{9,8},{10,9},{11,1... | collective-permute-start | bytes 983048 | tf_op jit(solution)/shard_map/ppermute | solution.py:83
  501.6 8.4 %collective-permute-start.7 = (bf16[4,64,640]{2,1,0:T(8,128)(2,1)S(1)}, bf16[4,64,640]{2,1,0:T(8,128)(2,1)S(1)}, u32[]{:S(2)}, u32[]{:S(2)}) collective-permute-start(bf16[4,64,640]{2,1,0:T(8,128)(2,1)S(1)} %fusion.48), channel_id=1, source_target_pairs={{0,1},{1,2},{2,3},{3,4},{4,5},{5,6},{6,7},{7,0},{8,9},{9,10},{10,1... | collective-permute-start | bytes 983048 | tf_op jit(solution)/shard_map/ppermute | solution.py:83
  506.1 5.2 collective-permute-start.18
  510.1 4.9 collective-permute-start.8
  511.3 3.9 collective-permute-start.19
  515.0 4.6 collective-permute-start.9
  515.2 4.5 collective-permute-start.20
  519.6 4.6 collective-permute-start.10
  524.2 4.6 collective-permute-start.21
  528.8 5.8 %collective-permute-start.22 = (bf16[64,1280]{1,0:T(8,128)(2,1)S(1)}, bf16[64,1280]{1,0:T(8,128)(2,1)S(1)}, u32[]{:S(2)}, u32[]{:S(2)}) collective-permute-start(bf16[64,1280]{1,0:T(8,128)(2,1)S(1)} %add_convert_fusion.1), channel_id=1, source_target_pairs={{0,128},{32,160},{64,192},{96,224},{128,0},{160,32},{192,64},{224,... | collective-permute-start | bytes 491528 | tf_op jit(solution)/shard_map/ppermute | solution.py:169
  534.7 21.6 %copy-start.5 = (bf16[32,128,64]{2,1,0:T(8,128)(2,1)S(1)}, bf16[32,128,64]{2,1,0:T(8,128)(2,1)}, u32[]{:S(2)}) copy-start(bf16[32,128,64]{2,1,0:T(8,128)(2,1)} %get-tuple-element.35) | copy-start | bytes 1572868
  534.7 22.9 %collective-permute-start.23 = (bf16[64,1280]{1,0:T(8,128)(2,1)S(1)}, bf16[64,1280]{1,0:T(8,128)(2,1)S(1)}, u32[]{:S(2)}, u32[]{:S(2)}) collective-permute-start(bf16[64,1280]{1,0:T(8,128)(2,1)S(1)} %add_convert_fusion), channel_id=1, source_target_pairs={{0,32},{32,0},{64,96},{96,64},{128,160},{160,128},{192,224},{224,1... | collective-permute-start | bytes 491528 | tf_op jit(solution)/shard_map/ppermute | solution.py:172
Sparse Core Ops, SparseCore 0:
  11.2 112.5 all-gather.1
where the time goes:
time: 572 us; the launch traced here: 566 us
  waiting for transfers between devices  258 us (45%)
  local copies, waits for them, and re-layouts  99.6 us (17%)
  matrix products  77.2 us (13%)
  starting transfers between devices  60.2 us (11%)
  other arithmetic  55.6 us (10%)
  between operations  15.4 us (3%)
    all_gather x1, waiting for transfers between devices, per_device(): w_full = lax.all_gather(w_local, 'seq', axis=0, tiled=True)  113 us
    all_to_all x1, waiting for transfers between devices, per_device(): lax.all_to_all(back_sent, 'seq', split_axis=0, concat_axis=0, tiled=True)  48.6 us
    all_to_all x1, waiting for transfers between devices, per_device(): lax.all_to_all(sent, 'seq', split_axis=0, concat_axis=1, tiled=True)[0]  46.1 us
    ppermute x20, waiting for transfers between devices, ring_reduce_scatter(): got = lax.ppermute(buf, 'seq', perm)  35.1 us
    ppermute x20, starting transfers between devices, ring_reduce_scatter(): got = lax.ppermute(buf, 'seq', perm)  27.9 us
    convert_element_type x20, other arithmetic, ring_reduce_scatter(): (got.astype(jnp.float32) + chunk(k + 1).astype(jnp.float32)).astype(jnp.b...  22.7 us
    concatenate x1, local copies, waits for them, and re-layouts, head_pass(): jnp.concatenate([grad_keys, grad_values], axis=-1)  16.1 us
    reshape x1, local copies, waits for them, and re-layouts, head_pass(): jnp.concatenate([grad_keys, grad_values], axis=-1)  16 us
  transfers between devices with their start and end apart: 27, of which 18 were waited for; matrix products, arithmetic and copies ran while one was open for 6% of the time, Pallas kernels for 0%

commit v1 on v0

--- a/solution.py
+++ b/solution.py
@@ -113,7 +113,10 @@
     )
     kv_pieces = jnp.repeat(paired.transpose(1, 0, 2), GROUP, axis=0)
     sent = jnp.concatenate([query_pieces, grad_pieces, kv_pieces], axis=2)
-    landed = lax.all_to_all(sent, "seq", split_axis=0, concat_axis=1, tiled=True)[0]
+    landed = jnp.concatenate(
+        lax.all_to_all(jnp.stack(jnp.split(sent, lax.axis_size("seq"), axis=0)), "seq", 0, 0),
+        axis=1,
+    )[0]
     head_q = landed[:, :HD]
     head_grad = landed[:, HD : 2 * HD]
     head_k = landed[:, 2 * HD : 3 * HD]

time: 572 us -> 588 us (1.028)
  local copies, waits for them, and re-layouts: 99.6 us -> 117 us
    unnamed x26 -> x55, local copies, waits for them, and re-layouts: 8.56 us -> 28.1 us
  transfers between devices with their start and end apart: 27 -> 27, of which waited for: 18 -> 17; matrix products, arithmetic and copies ran while one was open for 6% -> 6% of each run, Pallas kernels for 0% -> 0%
where the time goes in v1:
time: 588 us; the launch traced here: 582 us
  waiting for transfers between devices  257 us (44%)
  local copies, waits for them, and re-layouts  117 us (20%)
  matrix products  77 us (13%)
  starting transfers between devices  59.6 us (10%)
  other arithmetic  55.1 us (9%)
  between operations  15.7 us (3%)
    all_gather x1, waiting for transfers between devices, per_device(): w_full = lax.all_gather(w_local, 'seq', axis=0, tiled=True)  113 us
    all_to_all x1, waiting for transfers between devices, per_device(): lax.all_to_all(back_sent, 'seq', split_axis=0, concat_axis=0, tiled=True)  48.6 us
    all_to_all x1, waiting for transfers between devices, per_device(): lax.all_to_all(jnp.stack(jnp.split(sent, lax.axis_size('seq'), axis=0)),...  46.1 us
    ppermute x20, waiting for transfers between devices, ring_reduce_scatter(): got = lax.ppermute(buf, 'seq', perm)  34.6 us
    unnamed x55, local copies, waits for them, and re-layouts  28.1 us
    ppermute x20, starting transfers between devices, ring_reduce_scatter(): got = lax.ppermute(buf, 'seq', perm)  27.4 us
    convert_element_type x20, other arithmetic, ring_reduce_scatter(): (got.astype(jnp.float32) + chunk(k + 1).astype(jnp.float32)).astype(jnp.b...  22.7 us
    concatenate x1, local copies, waits for them, and re-layouts, head_pass(): jnp.concatenate([grad_keys, grad_values], axis=-1)  16.1 us
  transfers between devices with their start and end apart: 27, of which 17 were waited for; matrix products, arithmetic and copies ran while one was open for 6% of the time, Pallas kernels for 0%

profile of v1, /device:TPU:1, one launch (start us, length us, event | category | flops | bytes accessed | tf_op | source)
XLA Modules:
  0.0 581.6 jit_solution(11878209013802282436)
XLA Ops:
  7.2 1.8 pad_maximum_fusion.4
  10.9 112.9 %all-gather.2.cloned.1.call-done = bf16[2048,2560]{1,0:T(8,128)(2,1)} async-done(((bf16[64,2560]{1,0:T(8,128)(2,1)}), bf16[2048,2560]{1,0:T(8,128)(2,1)}) %all-gather.2.cloned.1.call-update) | async-done | bytes 10485776 | tf_op jit(solution)/shard_map/all_gather | solution.py:103
  123.7 6.9 %fusion.13 = bf16[128,2560]{0,1:T(8,128)(2,1)S(1)} fusion(bf16[2048,2560]{1,0:T(8,128)(2,1)} %all-gather.2.cloned.1.call-done, bf16[1,128,2048]{2,1,0:T(8,128)(2,1)S(1)} %copy-done), kind=kOutput, calls=%fused_computation.27 | convolution fusion | flops 1342504960 | bytes 11665408 | tf_op jit(solution)/shard_map/dot_general | solution.py:104
  152.8 5.7 all-to-all-start
  160.9 46.1 %all-to-all-done = bf16[32,1,128,256]{3,2,1,0:T(8,128)(2,1)S(1)} async-done(((bf16[32,1,128,256]{3,2,1,0:T(8,128)(2,1)}), bf16[32,1,128,256]{3,2,1,0:T(8,128)(2,1)S(1)}, u32[]{:S(2)}, u32[]{:S(2)}) %all-to-all-start) | async-done | bytes 2097184 | tf_op jit(solution)/shard_map/all_to_all | solution.py:117
  207.0 2.9 fusion.105
  211.5 2.9 gather_fusion
  214.3 6.2 %copy.131 = bf16[224,128,64]{1,0,2:T(8,128)(2,1)} copy(bf16[224,128,64]{1,2,0:T(8,128)(2,1)} %gather_fusion) | data formatting | bytes 7340032 | tf_op jit(solution)/shard_map/gather | solution.py:24
  220.5 7.8 %reshape.148 = bf16[32,896,64]{1,0,2:T(8,128)(2,1)} reshape(bf16[224,128,64]{1,0,2:T(8,128)(2,1)} %copy.131) | data formatting | bytes 7340032 | tf_op jit(solution)/shard_map/reshape | solution.py:24
  228.8 2.9 gather_fusion.1
  231.6 6.2 %copy.136 = bf16[224,128,64]{1,0,2:T(8,128)(2,1)} copy(bf16[224,128,64]{1,2,0:T(8,128)(2,1)} %gather_fusion.1) | data formatting | bytes 7340032 | tf_op jit(solution)/shard_map/gather | solution.py:25
  237.8 7.9 %reshape.150 = bf16[32,896,64]{1,0,2:T(8,128)(2,1)} reshape(bf16[224,128,64]{1,0,2:T(8,128)(2,1)} %copy.136) | data formatting | bytes 7340032 | tf_op jit(solution)/shard_map/reshape | solution.py:25
  245.7 10.8 %fusion.109 = (f32[32,128]{1,0:T(8,128)S(1)}, f32[32,128,896]{2,1,0:T(8,128)}) fusion(pred[896]{0:T(1024)(128)(4,1)S(1)} %broadcast_bitcast_fusion, bf16[32,128,64]{2,1,0:T(8,128)(2,1)S(1)} %bitcast.279, bf16[32,896,64]{1,0,2:T(8,128)(2,1)} %reshape.148), kind=kOutput, calls=%fused_computation.183 | convolution fusion | flops 484443008 | bytes 18891648 | tf_op jit(solution)/shard_map/sub | solution.py:31
  256.5 9.3 %fusion.31 = bf16[32,128,64]{1,2,0:T(8,128)(2,1)S(1)} fusion(bf16[32,896,64]{1,0,2:T(8,128)(2,1)} %reshape.150, f32[32,128,896]{2,1,0:T(8,128)} %get-tuple-element.44, f32[32,128]{1,0:T(8,128)S(1)} %get-tuple-element.43), kind=kOutput, calls=%fused_computation.42 | convolution fusion | flops 477364224 | bytes 18890752 | tf_op jit(solution)/shard_map/gqk,gke->gqe/dot_general | solution.py:34
  265.8 10.9 %multiply_reduce_fusion = (f32[32,128]{1,0:T(8,128)S(1)}, f32[32,128,896]{2,1,0:T(8,128)}) fusion(f32[32,128,896]{2,1,0:T(8,128)} %get-tuple-element.44, f32[32,128]{1,0:T(8,128)S(1)} %get-tuple-element.43, bf16[32,128,64]{2,1,0:T(8,128)(2,1)S(1)} %bitcast.290, bf16[32,896,64]{1,0,2:T(8,128)(2,1)} %reshape.150), kind=kOutput, calls=%fused_computation.9 | convolution fusion | flops 480768000 | bytes 33587200 | tf_op jit(solution)/shard_map/gqe,gke->gqk/dot_general | solution.py:37
  276.7 10.9 %multiply_convert_fusion.1 = bf16[32,128,896]{2,1,0:T(8,128)(2,1)S(1)} fusion(f32[32,128,896]{2,1,0:T(8,128)} %get-tuple-element.46, f32[32,128]{1,0:T(8,128)S(1)} %get-tuple-element.45, f32[32,128,896]{2,1,0:T(8,128)} %get-tuple-element.44, f32[32,128]{1,0:T(8,128)S(1)} %get-tuple-element.43), kind=kLoop, calls=%fused_computation.8 | loop fusion | flops 14680064 | bytes 36732928 | tf_op jit(solution)/shard_map/convert_element_type | solution.py:39
  287.6 3.4 fusion.28
  291.0 4.3 broadcast_multiply_fusion
  295.3 9.6 %fusion.9 = f32[32,896,64]{1,2,0:T(8,128)} fusion(bf16[32,128,64]{2,1,0:T(8,128)(2,1)S(1)} %bitcast.291, f32[32,128,896]{2,1,0:T(8,128)} %get-tuple-element.44, f32[32,128]{1,0:T(8,128)S(1)} %get-tuple-element.43), kind=kOutput, calls=%fused_computation.22 | convolution fusion | flops 477102080 | bytes 22560768 | tf_op jit(solution)/shard_map/gqk,gqe->gke/dot_general | solution.py:48
  306.5 2.5 copy.148
  309.0 10.6 %pad_maximum_fusion = f32[32,896,128]{1,2,0:T(8,128)} fusion(f32[32,896,64]{1,2,0:T(8,128)} %fusion.9, f32[32,896,64]{1,2,0:T(8,128)} %broadcast_multiply_fusion), kind=kLoop, calls=%fused_computation.7 | loop fusion | flops 3670016 | bytes 29360128 | tf_op jit(solution)/shard_map/concatenate | solution.py:49
  319.5 16.1 %copy.145 = f32[32,896,128]{2,1,0:T(8,128)} copy(f32[32,896,128]{1,2,0:T(8,128)} %pad_maximum_fusion) | data formatting | bytes 29360128 | tf_op jit(solution)/shard_map/concatenate | solution.py:49
  335.6 16.0 %reshape.152 = f32[224,16384]{1,0:T(8,128)} reshape(f32[32,896,128]{2,1,0:T(8,128)} %copy.145) | data formatting | bytes 29360128 | tf_op jit(solution)/shard_map/reshape | solution.py:49
  351.6 9.1 %fusion.22 = bf16[32,128,128]{2,0,1:T(8,128)(2,1)S(1)} fusion(s32[224]{0:T(256)S(1)} %eq.47, f32[224,16384]{1,0:T(8,128)} %reshape.152), kind=kOutput, calls=%fused_computation.39 | convolution fusion | flops 1409817600 | bytes 15729536 | tf_op jit(solution)/shard_map/dot_general | solution.py:56
  361.8 2.6 copy.149
  364.4 7.1 %all-to-all-start.1 = ((bf16[32,128,256]{2,1,0:T(8,128)(2,1)}), bf16[32,128,256]{2,1,0:T(8,128)(2,1)S(1)}, u32[]{:S(2)}, u32[]{:S(2)}) async-start(bf16[32,128,256]{2,1,0:T(8,128)(2,1)} %copy.149), calls=%async_computation.1 | async-start | bytes 4194304 | tf_op jit(solution)/shard_map/all_to_all | solution.py:137
  371.5 48.6 %all-to-all-done.1 = bf16[32,128,256]{2,1,0:T(8,128)(2,1)S(1)} async-done(((bf16[32,128,256]{2,1,0:T(8,128)(2,1)}), bf16[32,128,256]{2,1,0:T(8,128)(2,1)S(1)}, u32[]{:S(2)}, u32[]{:S(2)}) %all-to-all-start.1) | async-done | bytes 2097184 | tf_op jit(solution)/shard_map/all_to_all | solution.py:137
  420.9 1.9 fusion.104
  424.4 4.2 multiply_convert_fusion
  428.7 2.9 dynamic-slice_bitcast_fusion
  431.6 2.7 copy-done.1
  434.3 2.5 collective-permute-start
  436.8 8.6 %collective-permute-done = bf16[2048,1280]{1,0:T(8,128)(2,1)} collective-permute-done((bf16[2048,1280]{1,0:T(8,128)(2,1)}, bf16[2048,1280]{1,0:T(8,128)(2,1)}, u32[]{:S(2)}, u32[]{:S(2)}) %collective-permute-start) | collective-permute-done | bytes 5242912 | tf_op jit(solution)/shard_map/ppermute | solution.py:163
  445.4 5.4 fusion.5
  457.6 7.0 %collective-permute-done.1 = bf16[4,64,640]{2,1,0:T(8,128)(2,1)} collective-permute-done((bf16[4,64,640]{2,1,0:T(8,128)(2,1)}, bf16[4,64,640]{2,1,0:T(8,128)(2,1)}, u32[]{:S(2)}, u32[]{:S(2)}) %collective-permute-start.1) | collective-permute-done | bytes 327712 | tf_op jit(solution)/shard_map/ppermute | solution.py:83
  464.7 1.9 fusion.53
  466.8 1.8 fusion.46
  468.6 2.6 collective-permute-start.12
  471.2 5.1 collective-permute-done.2
  476.3 1.9 fusion.52
  479.9 2.7 collective-permute-start.13
  482.6 4.1 collective-permute-done.3
  486.8 1.9 fusion.51
  490.4 2.7 collective-permute-start.14
  493.1 3.0 collective-permute-done.4
  496.1 1.9 fusion.50
  498.0 1.8 fusion.43
  499.8 2.7 collective-permute-start.15
  502.4 3.0 collective-permute-done.5
  505.4 1.9 fusion.49
  509.1 2.7 collective-permute-start.16
  511.8 3.0 collective-permute-done.6
  514.8 1.9 fusion.48
  517.7 2.7 collective-permute-start.17
  520.5 3.6 collective-permute-done.7
  525.7 2.5 collective-permute-start.18
  528.3 2.0 collective-permute-done.8
  530.7 2.7 collective-permute-start.19
  535.3 2.7 collective-permute-start.20
  541.1 3.2 collective-permute-done.21
  544.3 2.8 collective-permute-start.22
  547.1 3.0 collective-permute-done.22
  550.2 12.9 %collective-permute-start.23 = (bf16[64,1280]{1,0:T(8,128)(2,1)S(1)}, bf16[64,1280]{1,0:T(8,128)(2,1)S(1)}, u32[]{:S(2)}, u32[]{:S(2)}) collective-permute-start(bf16[64,1280]{1,0:T(8,128)(2,1)S(1)} %add_convert_fusion), channel_id=1, source_target_pairs={{0,32},{32,0},{64,96},{96,64},{128,160},{160,128},{192,224},{224,1... | collective-permute-start | bytes 491528 | tf_op jit(solution)/shard_map/ppermute | solution.py:175
  563.0 8.5 %fusion.21 = bf16[1,128,2048]{2,1,0:T(8,128)(2,1)} fusion(bf16[2048,2560]{1,0:T(8,128)(2,1)} %all-gather.2.cloned.1.call-done, bf16[128,256]{0,1:T(8,128)(2,1)S(1)} %bitcast.295, bf16[128,256]{0,1:T(8,128)(2,1)S(1)} %bitcast.293, bf16[128,2048]{0,1:T(8,128)(2,1)} %bitcast.282), kind=kOutput, calls=%fused_computation.36 | convolution fusion | flops 1344405504 | bytes 11665408 | tf_op jit(solution)/shard_map/dot_general | solution.py:150
  (132 shorter events, 55.9 us)
Async XLA Ops:
  7.2 116.6 %copy-start = (bf16[1,128,2048]{2,1,0:T(8,128)(2,1)S(1)}, bf16[1,128,2048]{2,1,0:T(8,128)(2,1)}, u32[]{:S(2)}) copy-start(bf16[1,128,2048]{2,1,0:T(8,128)(2,1)} %param.7) | copy-start | bytes 1572868
  7.2 116.6 %all-gather.2.cloned.1.call-start = ((), (), s32[]{:S(2)}) async-start(), calls=%async_computation.2 | async-start | bytes 10813440 | tf_op jit(solution)/shard_map/all_gather | solution.py:103
  152.7 6.6 %copy-start.9 = (s32[32]{0:T(128)S(1)}, s32[32]{0:T(128)}, u32[]{:S(2)}) copy-start(s32[32]{0:T(128)} %param.12) | copy-start | bytes 388
  152.8 54.3 %all-to-all-start = ((bf16[32,1,128,256]{3,2,1,0:T(8,128)(2,1)}), bf16[32,1,128,256]{3,2,1,0:T(8,128)(2,1)S(1)}, u32[]{:S(2)}, u32[]{:S(2)}) async-start(bf16[32,1,128,256]{3,2,1,0:T(8,128)(2,1)} %fusion.62), calls=%async_computation | async-start | bytes 4194304 | tf_op jit(solution)/shard_map/all_to_all | solution.py:117
  220.5 7.8 %copy-start.6 = (bf16[4096,64]{1,0:T(8,128)(2,1)S(1)}, bf16[4096,64]{1,0:T(8,128)(2,1)}, u32[]{:S(2)}) copy-start(bf16[4096,64]{1,0:T(8,128)(2,1)} %get-tuple-element.31) | copy-start | bytes 1572868
  237.8 7.9 %copy-start.3 = (bf16[4096,64]{1,0:T(8,128)(2,1)S(1)}, bf16[4096,64]{1,0:T(8,128)(2,1)}, u32[]{:S(2)}) copy-start(bf16[4096,64]{1,0:T(8,128)(2,1)} %get-tuple-element.33) | copy-start | bytes 1572868
  256.5 9.3 %copy-start.8 = (bf16[4096,64]{1,0:T(8,128)(2,1)S(1)}, bf16[4096,64]{1,0:T(8,128)(2,1)}, u32[]{:S(2)}) copy-start(bf16[4096,64]{1,0:T(8,128)(2,1)} %get-tuple-element.34) | copy-start | bytes 1572868
  276.7 10.9 %copy-start.7 = (bf16[32,896,64]{1,0,2:T(8,128)(2,1)S(1)}, bf16[32,896,64]{1,0,2:T(8,128)(2,1)}, u32[]{:S(2)}) copy-start(bf16[32,896,64]{1,0,2:T(8,128)(2,1)} %reshape.148) | copy-start | bytes 11010052
  364.4 55.8 %all-to-all-start.1 = ((bf16[32,128,256]{2,1,0:T(8,128)(2,1)}), bf16[32,128,256]{2,1,0:T(8,128)(2,1)S(1)}, u32[]{:S(2)}, u32[]{:S(2)}) async-start(bf16[32,128,256]{2,1,0:T(8,128)(2,1)} %copy.149), calls=%async_computation.1 | async-start | bytes 4194304 | tf_op jit(solution)/shard_map/all_to_all | solution.py:137
  424.4 4.3 copy-start.4
  428.7 5.7 copy-start.1
  434.3 11.1 %collective-permute-start = (bf16[2048,1280]{1,0:T(8,128)(2,1)}, bf16[2048,1280]{1,0:T(8,128)(2,1)}, u32[]{:S(2)}, u32[]{:S(2)}) collective-permute-start(bf16[2048,1280]{1,0:T(8,128)(2,1)} %dynamic-slice_bitcast_fusion), channel_id=1, source_target_pairs={{0,32},{32,0},{64,96},{96,64},{128,160},{160,128},{192,224},{224,1... | collective-permute-start | bytes 15728648 | tf_op jit(solution)/shard_map/ppermute | solution.py:163
  452.0 1.5 copy-start.2
  454.2 10.5 %collective-permute-start.1 = (bf16[4,64,640]{2,1,0:T(8,128)(2,1)}, bf16[4,64,640]{2,1,0:T(8,128)(2,1)}, u32[]{:S(2)}, u32[]{:S(2)}) collective-permute-start(bf16[4,64,640]{2,1,0:T(8,128)(2,1)} %dynamic-slice_bitcast_fusion.2), channel_id=1, source_target_pairs={{0,1},{1,2},{2,3},{3,4},{4,5},{5,6},{6,7},{7,0},{8,9},{9,10},{10,1... | collective-permute-start | bytes 983048 | tf_op jit(solution)/shard_map/ppermute | solution.py:83
  456.2 10.6 %collective-permute-start.11 = (bf16[4,64,640]{2,1,0:T(8,128)(2,1)}, bf16[4,64,640]{2,1,0:T(8,128)(2,1)}, u32[]{:S(2)}, u32[]{:S(2)}) collective-permute-start(bf16[4,64,640]{2,1,0:T(8,128)(2,1)} %dynamic-slice_bitcast_fusion.1), channel_id=1, source_target_pairs={{1,0},{2,1},{3,2},{4,3},{5,4},{6,5},{7,6},{0,7},{9,8},{10,9},{11,1... | collective-permute-start | bytes 983048 | tf_op jit(solution)/shard_map/ppermute | solution.py:83
  466.6 9.7 %collective-permute-start.2 = (bf16[4,64,640]{2,1,0:T(8,128)(2,1)}, bf16[4,64,640]{2,1,0:T(8,128)(2,1)}, u32[]{:S(2)}, u32[]{:S(2)}) collective-permute-start(bf16[4,64,640]{2,1,0:T(8,128)(2,1)} %fusion.53), channel_id=1, source_target_pairs={{0,1},{1,2},{2,3},{3,4},{4,5},{5,6},{6,7},{7,0},{8,9},{9,10},{10,1... | collective-permute-start | bytes 983048 | tf_op jit(solution)/shard_map/ppermute | solution.py:83
  468.6 9.6 %collective-permute-start.12 = (bf16[4,64,640]{2,1,0:T(8,128)(2,1)}, bf16[4,64,640]{2,1,0:T(8,128)(2,1)}, u32[]{:S(2)}, u32[]{:S(2)}) collective-permute-start(bf16[4,64,640]{2,1,0:T(8,128)(2,1)} %fusion.46), channel_id=1, source_target_pairs={{1,0},{2,1},{3,2},{4,3},{5,4},{6,5},{7,6},{0,7},{9,8},{10,9},{11,1... | collective-permute-start | bytes 983048 | tf_op jit(solution)/shard_map/ppermute | solution.py:83
  478.2 8.6 %collective-permute-start.3 = (bf16[4,64,640]{2,1,0:T(8,128)(2,1)}, bf16[4,64,640]{2,1,0:T(8,128)(2,1)}, u32[]{:S(2)}, u32[]{:S(2)}) collective-permute-start(bf16[4,64,640]{2,1,0:T(8,128)(2,1)} %fusion.52), channel_id=1, source_target_pairs={{0,1},{1,2},{2,3},{3,4},{4,5},{5,6},{6,7},{7,0},{8,9},{9,10},{10,1... | collective-permute-start | bytes 983048 | tf_op jit(solution)/shard_map/ppermute | solution.py:83
  479.9 8.7 %collective-permute-start.13 = (bf16[4,64,640]{2,1,0:T(8,128)(2,1)}, bf16[4,64,640]{2,1,0:T(8,128)(2,1)}, u32[]{:S(2)}, u32[]{:S(2)}) collective-permute-start(bf16[4,64,640]{2,1,0:T(8,128)(2,1)} %fusion.45), channel_id=1, source_target_pairs={{1,0},{2,1},{3,2},{4,3},{5,4},{6,5},{7,6},{0,7},{9,8},{10,9},{11,1... | collective-permute-start | bytes 983048 | tf_op jit(solution)/shard_map/ppermute | solution.py:83
  488.6 7.5 %collective-permute-start.4 = (bf16[4,64,640]{2,1,0:T(8,128)(2,1)}, bf16[4,64,640]{2,1,0:T(8,128)(2,1)}, u32[]{:S(2)}, u32[]{:S(2)}) collective-permute-start(bf16[4,64,640]{2,1,0:T(8,128)(2,1)} %fusion.51), channel_id=1, source_target_pairs={{0,1},{1,2},{2,3},{3,4},{4,5},{5,6},{6,7},{7,0},{8,9},{9,10},{10,1... | collective-permute-start | bytes 983048 | tf_op jit(solution)/shard_map/ppermute | solution.py:83
  490.4 7.6 %collective-permute-start.14 = (bf16[4,64,640]{2,1,0:T(8,128)(2,1)}, bf16[4,64,640]{2,1,0:T(8,128)(2,1)}, u32[]{:S(2)}, u32[]{:S(2)}) collective-permute-start(bf16[4,64,640]{2,1,0:T(8,128)(2,1)} %fusion.44), channel_id=1, source_target_pairs={{1,0},{2,1},{3,2},{4,3},{5,4},{6,5},{7,6},{0,7},{9,8},{10,9},{11,1... | collective-permute-start | bytes 983048 | tf_op jit(solution)/shard_map/ppermute | solution.py:83
  498.0 7.5 %collective-permute-start.5 = (bf16[4,64,640]{2,1,0:T(8,128)(2,1)}, bf16[4,64,640]{2,1,0:T(8,128)(2,1)}, u32[]{:S(2)}, u32[]{:S(2)}) collective-permute-start(bf16[4,64,640]{2,1,0:T(8,128)(2,1)} %fusion.50), channel_id=1, source_target_pairs={{0,1},{1,2},{2,3},{3,4},{4,5},{5,6},{6,7},{7,0},{8,9},{9,10},{10,1... | collective-permute-start | bytes 983048 | tf_op jit(solution)/shard_map/ppermute | solution.py:83
  499.8 7.6 %collective-permute-start.15 = (bf16[4,64,640]{2,1,0:T(8,128)(2,1)}, bf16[4,64,640]{2,1,0:T(8,128)(2,1)}, u32[]{:S(2)}, u32[]{:S(2)}) collective-permute-start(bf16[4,64,640]{2,1,0:T(8,128)(2,1)} %fusion.43), channel_id=1, source_target_pairs={{1,0},{2,1},{3,2},{4,3},{5,4},{6,5},{7,6},{0,7},{9,8},{10,9},{11,1... | collective-permute-start | bytes 983048 | tf_op jit(solution)/shard_map/ppermute | solution.py:83
  507.3 7.5 %collective-permute-start.6 = (bf16[4,64,640]{2,1,0:T(8,128)(2,1)}, bf16[4,64,640]{2,1,0:T(8,128)(2,1)}, u32[]{:S(2)}, u32[]{:S(2)}) collective-permute-start(bf16[4,64,640]{2,1,0:T(8,128)(2,1)} %fusion.49), channel_id=1, source_target_pairs={{0,1},{1,2},{2,3},{3,4},{4,5},{5,6},{6,7},{7,0},{8,9},{9,10},{10,1... | collective-permute-start | bytes 983048 | tf_op jit(solution)/shard_map/ppermute | solution.py:83
  509.1 7.6 %collective-permute-start.16 = (bf16[4,64,640]{2,1,0:T(8,128)(2,1)}, bf16[4,64,640]{2,1,0:T(8,128)(2,1)}, u32[]{:S(2)}, u32[]{:S(2)}) collective-permute-start(bf16[4,64,640]{2,1,0:T(8,128)(2,1)} %fusion.42), channel_id=1, source_target_pairs={{1,0},{2,1},{3,2},{4,3},{5,4},{6,5},{7,6},{0,7},{9,8},{10,9},{11,1... | collective-permute-start | bytes 983048 | tf_op jit(solution)/shard_map/ppermute | solution.py:83
  516.7 7.5 %collective-permute-start.7 = (bf16[4,64,640]{2,1,0:T(8,128)(2,1)}, bf16[4,64,640]{2,1,0:T(8,128)(2,1)}, u32[]{:S(2)}, u32[]{:S(2)}) collective-permute-start(bf16[4,64,640]{2,1,0:T(8,128)(2,1)} %fusion.48), channel_id=1, source_target_pairs={{0,1},{1,2},{2,3},{3,4},{4,5},{5,6},{6,7},{7,0},{8,9},{9,10},{10,1... | collective-permute-start | bytes 983048 | tf_op jit(solution)/shard_map/ppermute | solution.py:83
  517.7 7.9 %collective-permute-start.17 = (bf16[4,64,640]{2,1,0:T(8,128)(2,1)S(1)}, bf16[4,64,640]{2,1,0:T(8,128)(2,1)S(1)}, u32[]{:S(2)}, u32[]{:S(2)}) collective-permute-start(bf16[4,64,640]{2,1,0:T(8,128)(2,1)S(1)} %fusion.41), channel_id=1, source_target_pairs={{1,0},{2,1},{3,2},{4,3},{5,4},{6,5},{7,6},{0,7},{9,8},{10,9},{11,1... | collective-permute-start | bytes 983048 | tf_op jit(solution)/shard_map/ppermute | solution.py:83
  525.3 5.0 collective-permute-start.8
  525.7 4.9 collective-permute-start.18
  530.3 4.8 collective-permute-start.9
  530.7 4.6 collective-permute-start.19
  535.2 4.6 collective-permute-start.10
  535.3 4.5 collective-permute-start.20
  539.8 4.5 collective-permute-start.21
  544.3 5.8 collective-permute-start.22
  550.1 21.4 %copy-start.5 = (bf16[32,128,64]{2,1,0:T(8,128)(2,1)S(1)}, bf16[32,128,64]{2,1,0:T(8,128)(2,1)}, u32[]{:S(2)}) copy-start(bf16[32,128,64]{2,1,0:T(8,128)(2,1)} %get-tuple-element.30) | copy-start | bytes 1572868
  550.2 22.8 %collective-permute-start.23 = (bf16[64,1280]{1,0:T(8,128)(2,1)S(1)}, bf16[64,1280]{1,0:T(8,128)(2,1)S(1)}, u32[]{:S(2)}, u32[]{:S(2)}) collective-permute-start(bf16[64,1280]{1,0:T(8,128)(2,1)S(1)} %add_convert_fusion), channel_id=1, source_target_pairs={{0,32},{32,0},{64,96},{96,64},{128,160},{160,128},{192,224},{224,1... | collective-permute-start | bytes 491528 | tf_op jit(solution)/shard_map/ppermute | solution.py:175
Sparse Core Ops, SparseCore 0:
  11.2 112.5 all-gather.1
